TPU v7x, 512 devices: a whole 4x8x8 slice. The times are simulated.
512 devices in a mesh: nodes: 128 (over z, y, core), rep: 4 (over x).
Axes of the slice: x: 4, y: 8, z: 8, core: 2. Of those that a mesh axis runs over, the one named last changes fastest.
Arguments:
- memory: float32 [65536, 512], P('nodes'), may hold values from -16 to 16
- last_tick: int32 [65536], P('nodes'), may hold values from 0 to 499
- src_local: int32 [65536], P(('nodes', 'rep')), may hold values from 0 to 511
- dst_owner: int32 [65536, 1], P(('nodes', 'rep')), may hold values from 0 to 127; in each aligned block of 128 rows (0 to 127, 128 to 255, ...) at most 2 rows name the same one
- dst_local: int32 [65536], P(('nodes', 'rep')), may hold values from 0 to 511
- event_tick: int32 [65536], P(('nodes', 'rep')), may hold values from 500 to 999
- nbr_owner: int32 [65536, 16, 1], P(('nodes', 'rep')), may hold values from 0 to 127; in each aligned block of 2048 rows (0 to 2047, 2048 to 4095, ..., all dimensions but the last counted through in order) at most 32 rows name the same one
- nbr_local: int32 [65536, 16], P(('nodes', 'rep')), may hold values from 0 to 511
- nbr_tick: int32 [65536, 16], P(('nodes', 'rep')), may hold values from 0 to 499
- freq: float32 [128], replicated, may hold values from 0.002 to 0.5
- phase: float32 [128], replicated, may hold values from -3.140625 to 3.140625
- w_message: bfloat16 [1152, 512], replicated, may hold values from -0.1875 to 0.1875
- gru_input: float32 [3, 512, 512], P(None, None, 'rep'), may hold values from -0.5 to 0.5
- gru_hidden: float32 [3, 512, 512], P(None, None, 'rep'), may hold values from -0.25 to 0.25
- gru_bias: float32 [4, 512], P(None, 'rep'), may hold values from -3 to 3
- w_query: bfloat16 [512, 512], replicated, may hold values from -1 to 1
- w_keyval_mem: bfloat16 [512, 1024], replicated, may hold values from -0.25 to 0.25
- w_keyval_time: bfloat16 [128, 1024], replicated, may hold values from -0.5 to 0.5
Outputs:
- new_memory: float32 [65536, 512], P('nodes', 'rep')
- embed: bfloat16 [65536, 512], P(('nodes', 'rep'))
Inputs may be any that keep to these rules, and one draw needn't show every extreme that they name: `dst_owner`: on one device no owner is named by more than 2 events. `nbr_owner`: on one device no owner is named by more than 32 neighbour entries.
All inputs are finite; a program needn't handle non-finite values.
Results may differ from a plain program's by a relative error of at most 0.012.
The roundings to bfloat16 on the way count: a program that leaves them out, or rounds other values in their place, can miss the bound.
Values may be sent and summed in bfloat16 or wider, within the bound.
No kernel may reach another device: no remote copies, remote signals or barrier semaphores. Data moves between devices by JAX's collectives and lax.ppermute only.
A program may use at most 128 MiB of HBM per device.

v0:
```python
import math
import jax
import jax.numpy as jnp
from jax import lax
from jax.sharding import PartitionSpec as P

HEADS = 8
HEAD_DIM = 64


def encode(gaps, freq, phase):
    return jnp.cos(gaps[..., None] * freq + phase)


def place(owner, groups, capacity):
    onehot = (owner[:, None] == jnp.arange(groups, dtype=jnp.int32)[None, :]).astype(jnp.int32)
    before = jnp.cumsum(onehot, axis=0) - onehot
    return owner * capacity + jnp.sum(before * onehot, axis=1)


def message_pair(src_rows, dst_rows, src_time, dst_time, w_message):
    count = src_rows.shape[0]
    stacked = jnp.concatenate(
        [
            jnp.concatenate([src_rows, dst_rows, src_time], axis=1),
            jnp.concatenate([dst_rows, src_rows, dst_time], axis=1),
        ],
        axis=0,
    )
    messages = jax.nn.silu(jnp.dot(stacked, w_message, preferred_element_type=jnp.float32)).astype(
        jnp.bfloat16
    )
    return (messages[:count], messages[count:])


def on_device(
    memory,
    last_tick,
    src_local,
    dst_owner,
    dst_local,
    event_tick,
    nbr_owner,
    nbr_local,
    nbr_tick,
    freq,
    phase,
    w_message,
    gru_input,
    gru_hidden,
    gru_bias,
    w_query,
    w_keyval_mem,
    w_keyval_time,
):
    groups = lax.axis_size("nodes")
    events = src_local.shape[0]
    rows_here = memory.shape[0]
    width_m = memory.shape[1]
    neighbours = nbr_local.shape[1]
    msg_width = w_message.shape[1]
    dst_cap = max(2, 2 * events // groups)
    nbr_cap = 2 * events * neighbours // groups
    dst_slot = place(dst_owner[:, 0], groups, dst_cap)
    nbr_slot = place(nbr_owner.reshape(-1), groups, nbr_cap)
    dst_ids = (
        jnp.full((groups * dst_cap,), -1, jnp.int32)
        .at[dst_slot]
        .set(dst_local)
        .reshape(groups, dst_cap)
    )
    nbr_ids = (
        jnp.full((groups * nbr_cap,), -1, jnp.int32)
        .at[nbr_slot]
        .set(nbr_local.reshape(-1))
        .reshape(groups, nbr_cap)
    )
    mem_half = memory.astype(jnp.bfloat16)
    near_rows = mem_half[src_local]
    near_ticks = last_tick[src_local]
    ticks = event_tick.astype(jnp.float32)
    got_dst, got_nbr = (
        lax.all_to_all(dst_ids, "nodes", split_axis=0, concat_axis=0, tiled=True),
        lax.all_to_all(nbr_ids, "nodes", split_axis=0, concat_axis=0, tiled=True),
    )
    safe_dst = jnp.maximum(got_dst, 0)
    reply_rows, reply_ticks = (
        lax.all_to_all(mem_half[safe_dst], "nodes", split_axis=0, concat_axis=0, tiled=True),
        lax.all_to_all(last_tick[safe_dst], "nodes", split_axis=0, concat_axis=0, tiled=True),
    )
    far_rows = reply_rows.reshape(-1, width_m)[dst_slot]
    far_ticks = reply_ticks.reshape(-1)[dst_slot]
    src_time = encode(ticks - near_ticks.astype(jnp.float32), freq, phase).astype(jnp.bfloat16)
    dst_time = encode(ticks - far_ticks.astype(jnp.float32), freq, phase).astype(jnp.bfloat16)
    msg_src, msg_dst = message_pair(near_rows, far_rows, src_time, dst_time, w_message)
    outgoing = (
        jnp.zeros((groups * dst_cap, msg_width), jnp.bfloat16)
        .at[dst_slot]
        .set(msg_dst)
        .reshape(groups, dst_cap, msg_width)
    )
    incoming = lax.all_to_all(outgoing, "nodes", split_axis=0, concat_axis=0, tiled=True)
    far_msgs = incoming.reshape(-1, msg_width)
    row_ids = jnp.arange(rows_here, dtype=jnp.int32)[:, None]
    hit_far = (row_ids == got_dst.reshape(1, -1)).astype(jnp.bfloat16)
    hit_near = (row_ids == src_local[None, :]).astype(jnp.bfloat16)
    sums = jnp.dot(hit_near, msg_src, preferred_element_type=jnp.float32) + jnp.dot(
        hit_far, far_msgs, preferred_element_type=jnp.float32
    )
    counts = jnp.sum(hit_near.astype(jnp.float32), axis=1) + jnp.sum(
        hit_far.astype(jnp.float32), axis=1
    )
    sums, counts = lax.psum((sums, counts), "rep")
    unit_width = gru_bias.shape[1]
    start = lax.axis_index("rep") * unit_width
    state_part = lax.dynamic_slice_in_dim(memory, start, unit_width, 1)
    mean = sums / jnp.maximum(counts, 1.0)[:, None]
    highest = lax.Precision.HIGHEST
    a_parts = jnp.einsum("rk,gku->gru", mean, gru_input, precision=highest)
    b_parts = jnp.einsum("rk,gku->gru", memory, gru_hidden, precision=highest)
    update = jax.nn.sigmoid(a_parts[0] + b_parts[0] + gru_bias[0])
    reset = jax.nn.sigmoid(a_parts[1] + b_parts[1] + gru_bias[1])
    cand = jnp.tanh(a_parts[2] + gru_bias[2] + reset * (b_parts[2] + gru_bias[3]))
    fresh = (1.0 - update) * cand + update * state_part
    new_part = jnp.where((counts > 0.0)[:, None], fresh, state_part)
    updated = lax.all_gather(new_part.astype(jnp.bfloat16), "rep", axis=1, tiled=True)
    served = updated[jnp.maximum(got_nbr, 0)]
    returned = lax.all_to_all(served, "nodes", split_axis=0, concat_axis=0, tiled=True)
    fetched = returned.reshape(-1, updated.shape[1])[nbr_slot]
    kv_mem = jnp.dot(fetched, w_keyval_mem, preferred_element_type=jnp.float32).astype(jnp.bfloat16)
    kv_mem = lax.optimization_barrier(kv_mem).astype(jnp.float32)
    gaps = ticks[:, None] - nbr_tick.astype(jnp.float32)
    time_enc = encode(gaps, freq, phase).reshape(-1, freq.shape[0]).astype(jnp.bfloat16)
    kv_time = jnp.dot(time_enc, w_keyval_time, preferred_element_type=jnp.float32)
    keyval = (kv_mem + kv_time).reshape(events, neighbours, 2, HEADS, HEAD_DIM)
    query = jnp.dot(updated[src_local], w_query, preferred_element_type=jnp.float32).astype(
        jnp.bfloat16
    )
    query = lax.optimization_barrier(query).astype(jnp.float32).reshape(events, HEADS, HEAD_DIM)
    scores = jnp.einsum("ehd,ejhd->ehj", query, keyval[:, :, 0]) / math.sqrt(HEAD_DIM)
    weights = jax.nn.softmax(scores, axis=-1)
    mixed = jnp.einsum("ehj,ejhd->ehd", weights, keyval[:, :, 1])
    embed = mixed.reshape(events, HEADS * HEAD_DIM).astype(jnp.bfloat16)
    return (new_part, embed)


def solution(mesh):
    placed = (
        P("nodes", None),
        P("nodes"),
        P(("nodes", "rep")),
        P(("nodes", "rep"), None),
        P(("nodes", "rep")),
        P(("nodes", "rep")),
        P(("nodes", "rep"), None, None),
        P(("nodes", "rep"), None),
        P(("nodes", "rep"), None),
        P(),
        P(),
        P(),
        P(None, None, "rep"),
        P(None, None, "rep"),
        P(None, "rep"),
        P(),
        P(),
        P(),
    )
    return jax.shard_map(
        on_device,
        mesh=mesh,
        in_specs=placed,
        out_specs=(P("nodes", "rep"), P(("nodes", "rep"), None)),
        check_vma=False,
    )
```

profile of v0, /device:TPU:41, one launch (start us, length us, event | category | flops | bytes accessed | tf_op | source)
XLA Modules:
  0.0 390.3 jit_solution(18406961669935850036)
XLA Ops:
  9.7 1.1 scatter_custom_fusion
  11.6 17.2 %all-to-all-start = ((s32[128,1,2]{2,1,0:T(1,128)}), s32[128,1,2]{2,1,0:T(1,128)S(1)}, u32[]{:S(2)}, u32[]{:S(2)}) async-start(s32[128,1,2]{2,1,0:T(1,128)} %bitcast.5), calls=%async_computation | async-start | bytes 131072 | tf_op jit(solution)/shard_map/all_to_all | solution.py:83
  32.7 4.2 %all-to-all-done = s32[128,1,2]{2,1,0:T(1,128)S(1)} async-done(((s32[128,1,2]{2,1,0:T(1,128)}), s32[128,1,2]{2,1,0:T(1,128)S(1)}, u32[]{:S(2)}, u32[]{:S(2)}) %all-to-all-start) | async-done | bytes 1056 | tf_op jit(solution)/shard_map/all_to_all | solution.py:83
  37.4 1.5 fusion.72
  39.1 1.9 gather_fusion.4
  41.8 9.6 %all-to-all-start.2 = ((s32[128,1,2]{2,1,0:T(1,128)}), s32[128,1,2]{2,1,0:T(1,128)S(1)}, u32[]{:S(2)}, u32[]{:S(2)}) async-start(s32[128,1,2]{2,1,0:T(1,128)} %bitcast.6), calls=%async_computation.2 | async-start | bytes 131072 | tf_op jit(solution)/shard_map/all_to_all | solution.py:89
  51.4 1.3 gather_fusion.3
  54.0 1.2 gather_fusion.1
  56.0 3.5 all-to-all-done.2
  59.5 10.2 %all-to-all-start.1 = ((bf16[128,2,512]{2,1,0:T(2,128)(2,1)}), bf16[128,2,512]{2,1,0:T(2,128)(2,1)S(1)}, u32[]{:S(2)}, u32[]{:S(2)}) async-start(bf16[128,2,512]{2,1,0:T(2,128)(2,1)} %reshape.151), calls=%async_computation.1 | async-start | bytes 524288 | tf_op jit(solution)/shard_map/all_to_all | solution.py:88
  70.7 1.3 gather_fusion.5
  72.5 9.4 %all-to-all-done.1 = bf16[128,2,512]{2,1,0:T(2,128)(2,1)S(1)} async-done(((bf16[128,2,512]{2,1,0:T(2,128)(2,1)}), bf16[128,2,512]{2,1,0:T(2,128)(2,1)S(1)}, u32[]{:S(2)}, u32[]{:S(2)}) %all-to-all-start.1) | async-done | bytes 262176 | tf_op jit(solution)/shard_map/all_to_all | solution.py:88
  83.4 1.1 scatter_custom_fusion.1
  85.4 8.8 %all-to-all-start.3 = ((bf16[128,2,512]{2,1,0:T(2,128)(2,1)}), bf16[128,2,512]{2,1,0:T(2,128)(2,1)S(1)}, u32[]{:S(2)}, u32[]{:S(2)}) async-start(bf16[128,2,512]{2,1,0:T(2,128)(2,1)} %reshape.135), calls=%async_computation.3 | async-start | bytes 524288 | tf_op jit(solution)/shard_map/all_to_all | solution.py:102
  94.3 8.1 %scatter_custom_fusion.2 = s32[4096]{0:T(1024)S(1)} fusion(s32[2048]{0:T(1024)S(1)} %bitcast.137, s32[2048]{0:T(1024)S(1)} %reshape.234, s32[]{:T(128)} %constant.15.clone.1), kind=kCustom, calls=%fused_computation.109 | custom fusion | bytes 16388 | tf_op jit(solution)/shard_map/scatter | solution.py:75
  103.0 3.0 convolution_bitcast_fusion
  107.0 14.2 %all-to-all-start.4 = ((s32[128,1,32]{2,1,0:T(1,128)}), s32[128,1,32]{2,1,0:T(1,128)}, u32[]{:S(2)}, u32[]{:S(2)}) async-start(s32[128,1,32]{2,1,0:T(1,128)} %bitcast.135), calls=%async_computation.4 | async-start | bytes 131072 | tf_op jit(solution)/shard_map/all_to_all | solution.py:84
  121.7 2.2 convolution_add_fusion
  124.3 8.7 %psum.14 = f32[512]{0:T(512)S(1)} all-reduce(f32[512]{0:T(512)S(1)} %add.150), channel_id=1, replica_groups=mesh['nodes'=128,'rep'=4] {'rep'}, use_global_device_ids=true, to_apply=%region_5.6 | all-reduce | flops 512 | bytes 4096 | tf_op jit(solution)/shard_map/psum | solution.py:113
  133.0 1.0 maximum_reduce_fusion
  134.1 46.1 %all-reduce.2.cloned.1.call-done = f32[512,512]{1,0:T(8,128)} async-done(((f32[512,512]{1,0:T(8,128)}), f32[512,512]{1,0:T(8,128)}) %all-reduce.2.cloned.1.call-update) | async-done | bytes 1048592 | tf_op jit(solution)/shard_map/psum | solution.py:113
  180.2 3.3 convolution_bitcast_fusion.1
  184.4 11.5 %all_gather.3 = bf16[512,512]{1,0:T(8,128)(2,1)S(1)} all-gather(bf16[512,128]{1,0:T(8,128)(2,1)S(1)} %get-tuple-element.10), channel_id=1, replica_groups=mesh['nodes'=128,'rep'=4] {'rep'}, dimensions={1}, use_global_device_ids=true | all-gather | bytes 655360 | tf_op jit(solution)/shard_map/all_gather | solution.py:126
  196.0 17.3 %gather_fusion.7 = bf16[4096,512]{1,0:T(8,128)(2,1)} fusion(bf16[512,512]{1,0:T(8,128)(2,1)S(1)} %all_gather.3, s32[4096]{0:T(1024)S(1)} %broadcast_clamp_fusion), kind=kCustom, calls=%fused_computation.7 | custom fusion | bytes 8404992 | tf_op jit(solution)/shard_map/gather | solution.py:127
  213.3 19.2 %all-to-all-start.5 = ((bf16[128,32,512]{2,1,0:T(8,128)(2,1)}), bf16[128,32,512]{2,1,0:T(8,128)(2,1)}, u32[]{:S(2)}, u32[]{:S(2)}) async-start(bf16[128,32,512]{2,1,0:T(8,128)(2,1)} %bitcast.132), calls=%async_computation.5 | async-start | bytes 8388608 | tf_op jit(solution)/shard_map/all_to_all | solution.py:128
  235.1 101.1 %all-to-all-done.5 = bf16[128,32,512]{2,1,0:T(8,128)(2,1)} async-done(((bf16[128,32,512]{2,1,0:T(8,128)(2,1)}), bf16[128,32,512]{2,1,0:T(8,128)(2,1)}, u32[]{:S(2)}, u32[]{:S(2)}) %all-to-all-start.5) | async-done | bytes 4194336 | tf_op jit(solution)/shard_map/all_to_all | solution.py:128
  336.2 10.3 %gather_fusion.8 = bf16[2048,512]{1,0:T(8,128)(2,1)S(1)} fusion(bf16[4096,512]{1,0:T(8,128)(2,1)} %bitcast.27, s32[2048]{0:T(1024)S(1)} %broadcast_clamp_fusion.1), kind=kCustom, calls=%fused_computation.8 | custom fusion | bytes 4202496 | tf_op jit(solution)/shard_map/gather | solution.py:129
  346.6 3.6 convolution_convert_fusion
  350.2 6.6 %convert_add_fusion = f32[2048,1024]{1,0:T(8,128)} fusion(bf16[2048,1024]{1,0:T(8,128)(2,1)S(1)} %convolution_convert_fusion, bf16[128,1024]{1,0:T(8,128)(2,1)S(1)} %copy-done.5, f32[128]{0:T(128)S(1)} %copy-done.13, f32[128]{0:T(128)S(1)} %copy-done.15, f32[2048]{0:T(1024)S(1)} %mul.102), kind=kOutput, calls=%fused_computation.19 | convolution fusion | flops 541851648 | bytes 12854272 | tf_op jit(solution)/shard_map/dot_general | solution.py:134
  356.9 13.4 %reshape.141 = f32[128,16,2,8,64]{4,3,2,1,0:T(8,128)} reshape(f32[2048,1024]{1,0:T(8,128)} %convert_add_fusion) | data formatting | bytes 16777216 | tf_op jit(solution)/shard_map/reshape | solution.py:135
  370.3 5.7 %fusion.4 = f32[128,8,16]{1,2,0:T(8,128)S(1)} fusion(f32[128,16,2,8,64]{4,3,2,1,0:T(8,128)} %reshape.141, f32[128,8,64]{2,1,0:T(8,128)S(1)} %copy-done.3), kind=kLoop, calls=%fused_computation.18 | loop fusion | flops 2080768 | bytes 4521984
  377.2 5.3 %fusion.2 = bf16[128,8,64]{2,1,0:T(8,128)(2,1)S(1)} fusion(f32[128,16,2,8,64]{4,3,2,1,0:T(8,128)} %reshape.141, f32[128,8,16]{1,2,0:T(8,128)S(1)} %copy.78), kind=kLoop, calls=%fused_computation.15 | loop fusion | flops 2031616 | bytes 4390912
  (112 shorter events, 22.7 us)
Async XLA Ops:
  7.2 75.6 %copy-start = (bf16[1152,512]{1,0:T(8,128)(2,1)S(1)}, bf16[1152,512]{1,0:T(8,128)(2,1)}, u32[]{:S(2)}) copy-start(bf16[1152,512]{1,0:T(8,128)(2,1)} %param.29) | copy-start | bytes 3538948
  7.2 31.8 %copy-start.1 = (s32[512]{0:T(512)S(1)}, s32[512]{0:T(512)}, u32[]{:S(2)}) copy-start(s32[512]{0:T(512)} %param.19) | copy-start | bytes 6148
  11.6 25.2 %all-to-all-start = ((s32[128,1,2]{2,1,0:T(1,128)}), s32[128,1,2]{2,1,0:T(1,128)S(1)}, u32[]{:S(2)}, u32[]{:S(2)}) async-start(s32[128,1,2]{2,1,0:T(1,128)} %bitcast.5), calls=%async_computation | async-start | bytes 131072 | tf_op jit(solution)/shard_map/all_to_all | solution.py:83
  39.0 13.9 %copy-start.9 = (s32[128,16]{0,1:T(8,128)S(1)}, s32[128,16]{0,1:T(8,128)}, u32[]{:S(2)}) copy-start(s32[128,16]{0,1:T(8,128)} %param.25) | copy-start | bytes 24580
  39.0 14.0 %copy-start.2 = (f32[512,512]{1,0:T(8,128)S(1)}, f32[512,512]{1,0:T(8,128)}, u32[]{:S(2)}) copy-start(f32[512,512]{1,0:T(8,128)} %param.18) | copy-start | bytes 3145732
  41.0 30.9 %copy-start.18 = (s32[128]{0:T(128)S(1)}, s32[128]{0:T(128)}, u32[]{:S(2)}) copy-start(s32[128]{0:T(128)} %param.23) | copy-start | bytes 1540
  41.0 30.9 %copy-start.12 = (f32[128]{0:T(128)S(1)}, f32[128]{0:T(128)}, u32[]{:S(2)}) copy-start(f32[128]{0:T(128)} %param.28) | copy-start | bytes 1540
  41.0 30.9 %copy-start.14 = (f32[128]{0:T(128)S(1)}, f32[128]{0:T(128)}, u32[]{:S(2)}) copy-start(f32[128]{0:T(128)} %param.27) | copy-start | bytes 1540
  41.8 17.7 %all-to-all-start.2 = ((s32[128,1,2]{2,1,0:T(1,128)}), s32[128,1,2]{2,1,0:T(1,128)S(1)}, u32[]{:S(2)}, u32[]{:S(2)}) async-start(s32[128,1,2]{2,1,0:T(1,128)} %bitcast.6), calls=%async_computation.2 | async-start | bytes 131072 | tf_op jit(solution)/shard_map/all_to_all | solution.py:89
  51.4 1.8 copy-start.11
  59.5 22.4 %all-to-all-start.1 = ((bf16[128,2,512]{2,1,0:T(2,128)(2,1)}), bf16[128,2,512]{2,1,0:T(2,128)(2,1)S(1)}, u32[]{:S(2)}, u32[]{:S(2)}) async-start(bf16[128,2,512]{2,1,0:T(2,128)(2,1)} %reshape.151), calls=%async_computation.1 | async-start | bytes 524288 | tf_op jit(solution)/shard_map/all_to_all | solution.py:88
  83.4 37.8 %copy-start.6 = (bf16[256,512]{1,0:T(8,128)(2,1)}, bf16[256,512]{1,0:T(8,128)(2,1)S(1)}, u32[]{:S(2)}) copy-start(bf16[256,512]{1,0:T(8,128)(2,1)S(1)} %multiply_convert_fusion) | copy-start | bytes 786436
  83.4 38.3 %copy-start.16 = (s32[128]{0:T(128)S(1)}, s32[128]{0:T(128)}, u32[]{:S(2)}) copy-start(s32[128]{0:T(128)} %param.20) | copy-start | bytes 1540
  85.4 38.6 %copy-start.17 = (f32[4,128]{1,0:T(4,128)S(1)}, f32[4,128]{1,0:T(4,128)}, u32[]{:S(2)}) copy-start(f32[4,128]{1,0:T(4,128)} %param.32) | copy-start | bytes 6148
  85.4 21.6 %all-to-all-start.3 = ((bf16[128,2,512]{2,1,0:T(2,128)(2,1)}), bf16[128,2,512]{2,1,0:T(2,128)(2,1)S(1)}, u32[]{:S(2)}, u32[]{:S(2)}) async-start(bf16[128,2,512]{2,1,0:T(2,128)(2,1)} %reshape.135), calls=%async_computation.3 | async-start | bytes 524288 | tf_op jit(solution)/shard_map/all_to_all | solution.py:102
  94.3 8.1 %copy-start.7 = (s32[2048,1]{0,1:T(1,128)}, s32[2048,1]{0,1:T(1,128)S(1)}, u32[]{:S(2)}) copy-start(s32[2048,1]{0,1:T(1,128)S(1)} %compare_select_fusion) | copy-start | bytes 24580
  107.0 26.0 %all-to-all-start.4 = ((s32[128,1,32]{2,1,0:T(1,128)}), s32[128,1,32]{2,1,0:T(1,128)}, u32[]{:S(2)}, u32[]{:S(2)}) async-start(s32[128,1,32]{2,1,0:T(1,128)} %bitcast.135), calls=%async_computation.4 | async-start | bytes 131072 | tf_op jit(solution)/shard_map/all_to_all | solution.py:84
  121.3 58.9 %all-reduce.2.cloned.1.call-start = ((), (), s32[]{:S(2)}) async-start(), calls=%async_computation.6 | async-start | bytes 2097152 | tf_op jit(solution)/shard_map/psum | solution.py:113
  213.3 19.2 %copy-start.19 = (s32[128]{0:T(128)S(1)}, s32[128]{0:T(128)}, u32[]{:S(2)}) copy-start(s32[128]{0:T(128)} %param.23) | copy-start | bytes 1540
  213.3 19.2 %copy-start.10 = (s32[128,16]{0,1:T(8,128)S(1)}, s32[128,16]{0,1:T(8,128)}, u32[]{:S(2)}) copy-start(s32[128,16]{0,1:T(8,128)} %param.26) | copy-start | bytes 24580
  213.3 19.5 %copy-start.8 = (s32[2048,1]{0,1:T(1,128)S(1)}, s32[2048,1]{0,1:T(1,128)}, u32[]{:S(2)}) copy-start(s32[2048,1]{0,1:T(1,128)} %copy-done.7) | copy-start | bytes 24580
  213.3 20.4 %copy-start.4 = (bf16[512,512]{1,0:T(8,128)(2,1)S(1)}, bf16[512,512]{1,0:T(8,128)(2,1)}, u32[]{:S(2)}) copy-start(bf16[512,512]{1,0:T(8,128)(2,1)} %param.33) | copy-start | bytes 1572868
  213.3 122.9 %all-to-all-start.5 = ((bf16[128,32,512]{2,1,0:T(8,128)(2,1)}), bf16[128,32,512]{2,1,0:T(8,128)(2,1)}, u32[]{:S(2)}, u32[]{:S(2)}) async-start(bf16[128,32,512]{2,1,0:T(8,128)(2,1)} %bitcast.132), calls=%async_computation.5 | async-start | bytes 8388608 | tf_op jit(solution)/shard_map/all_to_all | solution.py:128
  346.6 3.6 copy-start.5
  346.6 3.6 copy-start.13
  346.6 3.6 copy-start.15
  356.8 13.4 %copy-start.3 = (f32[128,8,64]{2,1,0:T(8,128)S(1)}, f32[128,8,64]{2,1,0:T(8,128)}, u32[]{:S(2)}) copy-start(f32[128,8,64]{2,1,0:T(8,128)} %copy.77) | copy-start | bytes 786436
Sparse Core Ops, SparseCore 0:
  124.4 55.7 all-reduce.1
where the time goes:
time: 392 us; the launch traced here: 390 us
  waiting for transfers between devices  164 us (42%)
  starting transfers between devices  79.3 us (20%)
  local copies, waits for them, and re-layouts  70.6 us (18%)
  other arithmetic  21.3 us (5%)
  blocking collectives  20.3 us (5%)
  matrix products  19.8 us (5%)
  between operations  14.7 us (4%)
    all_to_all x1, waiting for transfers between devices, on_device(): lax.all_to_all(served, 'nodes', split_axis=0, concat_axis=0, tiled=True)  101 us
    psum x1, waiting for transfers between devices, on_device(): sums, counts = lax.psum((sums, counts), 'rep')  46.1 us
    all_to_all x1, starting transfers between devices, on_device(): lax.all_to_all(served, 'nodes', split_axis=0, concat_axis=0, tiled=True)  19.2 us
    gather x1, local copies, waits for them, and re-layouts, on_device(): served = updated[jnp.maximum(got_nbr, 0)]  17.3 us
    all_to_all x1, starting transfers between devices, on_device(): lax.all_to_all(dst_ids, 'nodes', split_axis=0, concat_axis=0, tiled=True)  17.2 us
    all_to_all x1, starting transfers between devices, on_device(): lax.all_to_all(nbr_ids, 'nodes', split_axis=0, concat_axis=0, tiled=True)  14.2 us
    reshape x1, local copies, waits for them, and re-layouts, on_device(): keyval = (kv_mem + kv_time).reshape(events, neighbours, 2, HEADS, HEAD_DIM)  13.4 us
    all_gather x1, blocking collectives, on_device(): lax.all_gather(new_part.astype(jnp.bfloat16), 'rep', axis=1, tiled=True)  11.5 us
  transfers between devices with their start and end apart: 7, of which 5 were waited for; matrix products, arithmetic and copies ran while one was open for 8% of the time, Pallas kernels for 0%

commit v1 on v0

--- a/solution.py
+++ b/solution.py
@@ -123,7 +123,12 @@
     cand = jnp.tanh(a_parts[2] + gru_bias[2] + reset * (b_parts[2] + gru_bias[3]))
     fresh = (1.0 - update) * cand + update * state_part
     new_part = jnp.where((counts > 0.0)[:, None], fresh, state_part)
-    updated = lax.all_gather(new_part.astype(jnp.bfloat16), "rep", axis=1, tiled=True)
+    updated = jnp.concatenate(
+        lax.all_to_all(
+            jnp.stack([new_part.astype(jnp.bfloat16)] * lax.axis_size("rep")), "rep", 0, 0
+        ),
+        axis=1,
+    )
     served = updated[jnp.maximum(got_nbr, 0)]
     returned = lax.all_to_all(served, "nodes", split_axis=0, concat_axis=0, tiled=True)
     fetched = returned.reshape(-1, updated.shape[1])[nbr_slot]

time: 392 us -> 386 us (0.985)
  blocking collectives: 20.3 us -> 8.71 us
  waiting for transfers between devices: 164 us -> 173 us
    all_gather x1 -> x0, blocking collectives: 11.5 us -> none  [on_device(): lax.all_gather(new_part.astype(jnp.bfloat16), 'rep', axis=1, tiled=True)]
    all_to_all x0 -> x1, waiting for transfers between devices: none -> 6.6 us  [on_device(): lax.all_to_all(jnp.stack([new_part.astype(jnp.bfloat16)] * lax.axis_size(...]
  transfers between devices with their start and end apart: 7 -> 8, of which waited for: 5 -> 7; matrix products, arithmetic and copies ran while one was open for 8% -> 8% of each run, Pallas kernels for 0% -> 0%
where the time goes in v1:
time: 386 us; the launch traced here: 384 us
  waiting for transfers between devices  173 us (45%)
  starting transfers between devices  78.3 us (20%)
  local copies, waits for them, and re-layouts  70.6 us (18%)
  other arithmetic  20.1 us (5%)
  matrix products  18.9 us (5%)
  between operations  14.6 us (4%)
  blocking collectives  8.71 us (2%)
    all_to_all x1, waiting for transfers between devices, on_device(): lax.all_to_all(served, 'nodes', split_axis=0, concat_axis=0, tiled=True)  101 us
    psum x1, waiting for transfers between devices, on_device(): sums, counts = lax.psum((sums, counts), 'rep')  45.2 us
    all_to_all x1, starting transfers between devices, on_device(): lax.all_to_all(served, 'nodes', split_axis=0, concat_axis=0, tiled=True)  18.4 us
    gather x1, local copies, waits for them, and re-layouts, on_device(): served = updated[jnp.maximum(got_nbr, 0)]  17.3 us
    all_to_all x1, starting transfers between devices, on_device(): lax.all_to_all(dst_ids, 'nodes', split_axis=0, concat_axis=0, tiled=True)  17.2 us
    reshape x1, local copies, waits for them, and re-layouts, on_device(): keyval = (kv_mem + kv_time).reshape(events, neighbours, 2, HEADS, HEAD_DIM)  13.4 us
    unnamed x2, other arithmetic  10.9 us
    all_to_all x1, starting transfers between devices, on_device(): lax.all_to_all(nbr_ids, 'nodes', split_axis=0, concat_axis=0, tiled=True)  10.7 us
  transfers between devices with their start and end apart: 8, of which 7 were waited for; matrix products, arithmetic and copies ran while one was open for 8% of the time, Pallas kernels for 0%

profile of v1, /device:TPU:41, one launch (start us, length us, event | category | flops | bytes accessed | tf_op | source)
XLA Modules:
  0.0 384.4 jit_solution(16366311658961566390)
XLA Ops:
  9.7 1.1 scatter_custom_fusion
  11.6 17.2 %all-to-all-start = ((s32[128,1,2]{2,1,0:T(1,128)}), s32[128,1,2]{2,1,0:T(1,128)S(1)}, u32[]{:S(2)}, u32[]{:S(2)}) async-start(s32[128,1,2]{2,1,0:T(1,128)} %bitcast.5), calls=%async_computation | async-start | bytes 131072 | tf_op jit(solution)/shard_map/all_to_all | solution.py:83
  32.7 4.2 %all-to-all-done = s32[128,1,2]{2,1,0:T(1,128)S(1)} async-done(((s32[128,1,2]{2,1,0:T(1,128)}), s32[128,1,2]{2,1,0:T(1,128)S(1)}, u32[]{:S(2)}, u32[]{:S(2)}) %all-to-all-start) | async-done | bytes 1056 | tf_op jit(solution)/shard_map/all_to_all | solution.py:83
  38.7 1.9 gather_fusion.4
  41.4 9.6 %all-to-all-start.2 = ((s32[128,1,2]{2,1,0:T(1,128)}), s32[128,1,2]{2,1,0:T(1,128)S(1)}, u32[]{:S(2)}, u32[]{:S(2)}) async-start(s32[128,1,2]{2,1,0:T(1,128)} %bitcast.6), calls=%async_computation.2 | async-start | bytes 131072 | tf_op jit(solution)/shard_map/all_to_all | solution.py:89
  51.0 1.3 gather_fusion.3
  53.6 1.2 gather_fusion.1
  55.6 3.5 all-to-all-done.2
  59.0 10.3 %all-to-all-start.1 = ((bf16[128,2,512]{2,1,0:T(2,128)(2,1)}), bf16[128,2,512]{2,1,0:T(2,128)(2,1)S(1)}, u32[]{:S(2)}, u32[]{:S(2)}) async-start(bf16[128,2,512]{2,1,0:T(2,128)(2,1)} %reshape.161), calls=%async_computation.1 | async-start | bytes 524288 | tf_op jit(solution)/shard_map/all_to_all | solution.py:88
  70.3 1.3 gather_fusion.5
  72.2 9.3 %all-to-all-done.1 = bf16[128,2,512]{2,1,0:T(2,128)(2,1)S(1)} async-done(((bf16[128,2,512]{2,1,0:T(2,128)(2,1)}), bf16[128,2,512]{2,1,0:T(2,128)(2,1)S(1)}, u32[]{:S(2)}, u32[]{:S(2)}) %all-to-all-start.1) | async-done | bytes 262176 | tf_op jit(solution)/shard_map/all_to_all | solution.py:88
  83.0 1.1 scatter_custom_fusion.1
  85.0 8.7 %all-to-all-start.3 = ((bf16[128,2,512]{2,1,0:T(2,128)(2,1)}), bf16[128,2,512]{2,1,0:T(2,128)(2,1)S(1)}, u32[]{:S(2)}, u32[]{:S(2)}) async-start(bf16[128,2,512]{2,1,0:T(2,128)(2,1)} %reshape.143), calls=%async_computation.3 | async-start | bytes 524288 | tf_op jit(solution)/shard_map/all_to_all | solution.py:102
  93.7 8.1 %scatter_custom_fusion.2 = s32[4096]{0:T(1024)S(1)} fusion(s32[2048]{0:T(1024)S(1)} %bitcast.142, s32[2048]{0:T(1024)S(1)} %reshape.244, s32[]{:T(128)} %constant.15.clone.1), kind=kCustom, calls=%fused_computation.110 | custom fusion | bytes 16388 | tf_op jit(solution)/shard_map/scatter | solution.py:75
  102.7 3.1 all-to-all-done.3
  105.9 10.7 %all-to-all-start.5 = ((s32[128,1,32]{2,1,0:T(1,128)}), s32[128,1,32]{2,1,0:T(1,128)S(1)}, u32[]{:S(2)}, u32[]{:S(2)}) async-start(s32[128,1,32]{2,1,0:T(1,128)} %bitcast.26), calls=%async_computation.5 | async-start | bytes 131072 | tf_op jit(solution)/shard_map/all_to_all | solution.py:84
  117.0 1.3 convolution_add_fusion
  118.4 3.0 convolution_bitcast_fusion
  121.5 8.7 %psum.14 = f32[512]{0:T(512)S(1)} all-reduce(f32[512]{0:T(512)S(1)} %add.150), channel_id=1, replica_groups=mesh['nodes'=128,'rep'=4] {'rep'}, use_global_device_ids=true, to_apply=%region_5.6 | all-reduce | flops 512 | bytes 4096 | tf_op jit(solution)/shard_map/psum | solution.py:113
  130.2 45.2 %all-reduce.2.cloned.1.call-done = f32[512,512]{1,0:T(8,128)} async-done(((f32[512,512]{1,0:T(8,128)}), f32[512,512]{1,0:T(8,128)}) %all-reduce.2.cloned.1.call-update) | async-done | bytes 1048592 | tf_op jit(solution)/shard_map/psum | solution.py:113
  175.4 3.3 convolution_bitcast_fusion.1
  180.5 3.5 all-to-all-start.4
  184.3 6.6 %all-to-all-done.4 = bf16[4,512,128]{2,1,0:T(8,128)(2,1)S(1)} async-done(((bf16[4,512,128]{2,1,0:T(8,128)(2,1)}), bf16[4,512,128]{2,1,0:T(8,128)(2,1)S(1)}, u32[]{:S(2)}, u32[]{:S(2)}) %all-to-all-start.4) | async-done | bytes 524320 | tf_op jit(solution)/shard_map/all_to_all | solution.py:127
  191.0 17.3 %gather_fusion.7 = bf16[4096,512]{1,0:T(8,128)(2,1)} fusion(bf16[512,512]{1,0:T(8,128)(2,1)S(1)} %copy_bitcast_fusion, s32[4096]{0:T(1024)S(1)} %broadcast_clamp_fusion), kind=kCustom, calls=%fused_computation.7 | custom fusion | bytes 8404992 | tf_op jit(solution)/shard_map/gather | solution.py:132
  208.3 18.4 %all-to-all-start.6 = ((bf16[128,32,512]{2,1,0:T(8,128)(2,1)}), bf16[128,32,512]{2,1,0:T(8,128)(2,1)}, u32[]{:S(2)}, u32[]{:S(2)}) async-start(bf16[128,32,512]{2,1,0:T(8,128)(2,1)} %bitcast.138), calls=%async_computation.6 | async-start | bytes 8388608 | tf_op jit(solution)/shard_map/all_to_all | solution.py:133
  229.1 101.3 %all-to-all-done.6 = bf16[128,32,512]{2,1,0:T(8,128)(2,1)} async-done(((bf16[128,32,512]{2,1,0:T(8,128)(2,1)}), bf16[128,32,512]{2,1,0:T(8,128)(2,1)}, u32[]{:S(2)}, u32[]{:S(2)}) %all-to-all-start.6) | async-done | bytes 4194336 | tf_op jit(solution)/shard_map/all_to_all | solution.py:133
  330.4 10.3 %gather_fusion.8 = bf16[2048,512]{1,0:T(8,128)(2,1)S(1)} fusion(bf16[4096,512]{1,0:T(8,128)(2,1)} %bitcast.28, s32[2048]{0:T(1024)S(1)} %broadcast_clamp_fusion.1), kind=kCustom, calls=%fused_computation.8 | custom fusion | bytes 4202496 | tf_op jit(solution)/shard_map/gather | solution.py:134
  340.7 3.6 convolution_convert_fusion
  344.3 6.6 %convert_add_fusion = f32[2048,1024]{1,0:T(8,128)} fusion(bf16[2048,1024]{1,0:T(8,128)(2,1)S(1)} %convolution_convert_fusion, bf16[128,1024]{1,0:T(8,128)(2,1)S(1)} %copy-done.5, f32[128]{0:T(128)S(1)} %copy-done.8, f32[128]{0:T(128)S(1)} %copy-done.9, f32[2048]{0:T(1024)S(1)} %mul.102), kind=kOutput, calls=%fused_computation.19 | convolution fusion | flops 541851648 | bytes 12854272 | tf_op jit(solution)/shard_map/dot_general | solution.py:139
  351.0 13.4 %reshape.151 = f32[128,16,2,8,64]{4,3,2,1,0:T(8,128)} reshape(f32[2048,1024]{1,0:T(8,128)} %convert_add_fusion) | data formatting | bytes 16777216 | tf_op jit(solution)/shard_map/reshape | solution.py:140
  364.4 5.7 %fusion.4 = f32[128,8,16]{1,2,0:T(8,128)S(1)} fusion(f32[128,16,2,8,64]{4,3,2,1,0:T(8,128)} %reshape.151, f32[128,8,64]{2,1,0:T(8,128)S(1)} %copy-done.3), kind=kLoop, calls=%fused_computation.18 | loop fusion | flops 2080768 | bytes 4521984
  371.3 5.3 %fusion.2 = bf16[128,8,64]{2,1,0:T(8,128)(2,1)S(1)} fusion(f32[128,16,2,8,64]{4,3,2,1,0:T(8,128)} %reshape.151, f32[128,8,16]{1,2,0:T(8,128)S(1)} %copy.80), kind=kLoop, calls=%fused_computation.15 | loop fusion | flops 2031616 | bytes 4390912
  (101 shorter events, 24.0 us)
Async XLA Ops:
  7.2 75.2 %copy-start = (bf16[1152,512]{1,0:T(8,128)(2,1)S(1)}, bf16[1152,512]{1,0:T(8,128)(2,1)}, u32[]{:S(2)}) copy-start(bf16[1152,512]{1,0:T(8,128)(2,1)} %param.29) | copy-start | bytes 3538948
  7.2 31.4 %copy-start.1 = (s32[512]{0:T(512)S(1)}, s32[512]{0:T(512)}, u32[]{:S(2)}) copy-start(s32[512]{0:T(512)} %param.19) | copy-start | bytes 6148
  11.6 25.2 %all-to-all-start = ((s32[128,1,2]{2,1,0:T(1,128)}), s32[128,1,2]{2,1,0:T(1,128)S(1)}, u32[]{:S(2)}, u32[]{:S(2)}) async-start(s32[128,1,2]{2,1,0:T(1,128)} %bitcast.5), calls=%async_computation | async-start | bytes 131072 | tf_op jit(solution)/shard_map/all_to_all | solution.py:83
  38.6 13.9 %copy-start.6 = (s32[128,16]{0,1:T(8,128)S(1)}, s32[128,16]{0,1:T(8,128)}, u32[]{:S(2)}) copy-start(s32[128,16]{0,1:T(8,128)} %param.25) | copy-start | bytes 24580
  38.6 14.0 %copy-start.2 = (f32[512,512]{1,0:T(8,128)S(1)}, f32[512,512]{1,0:T(8,128)}, u32[]{:S(2)}) copy-start(f32[512,512]{1,0:T(8,128)} %param.18) | copy-start | bytes 3145732
  40.6 31.0 %copy-start.12 = (s32[128]{0:T(128)S(1)}, s32[128]{0:T(128)}, u32[]{:S(2)}) copy-start(s32[128]{0:T(128)} %param.23) | copy-start | bytes 1540
  40.6 31.0 %copy-start.8 = (f32[128]{0:T(128)S(1)}, f32[128]{0:T(128)}, u32[]{:S(2)}) copy-start(f32[128]{0:T(128)} %param.28) | copy-start | bytes 1540
  40.6 31.0 %copy-start.9 = (f32[128]{0:T(128)S(1)}, f32[128]{0:T(128)}, u32[]{:S(2)}) copy-start(f32[128]{0:T(128)} %param.27) | copy-start | bytes 1540
  41.4 17.6 %all-to-all-start.2 = ((s32[128,1,2]{2,1,0:T(1,128)}), s32[128,1,2]{2,1,0:T(1,128)S(1)}, u32[]{:S(2)}, u32[]{:S(2)}) async-start(s32[128,1,2]{2,1,0:T(1,128)} %bitcast.6), calls=%async_computation.2 | async-start | bytes 131072 | tf_op jit(solution)/shard_map/all_to_all | solution.py:89
  59.0 22.4 %all-to-all-start.1 = ((bf16[128,2,512]{2,1,0:T(2,128)(2,1)}), bf16[128,2,512]{2,1,0:T(2,128)(2,1)S(1)}, u32[]{:S(2)}, u32[]{:S(2)}) async-start(bf16[128,2,512]{2,1,0:T(2,128)(2,1)} %reshape.161), calls=%async_computation.1 | async-start | bytes 524288 | tf_op jit(solution)/shard_map/all_to_all | solution.py:88
  82.4 20.1 %copy-start.10 = (s32[128]{0:T(128)S(1)}, s32[128]{0:T(128)}, u32[]{:S(2)}) copy-start(s32[128]{0:T(128)} %param.20) | copy-start | bytes 1540
  83.0 35.4 %copy-start.11 = (f32[4,128]{1,0:T(4,128)S(1)}, f32[4,128]{1,0:T(4,128)}, u32[]{:S(2)}) copy-start(f32[4,128]{1,0:T(4,128)} %param.32) | copy-start | bytes 6148
  85.0 20.9 %all-to-all-start.3 = ((bf16[128,2,512]{2,1,0:T(2,128)(2,1)}), bf16[128,2,512]{2,1,0:T(2,128)(2,1)S(1)}, u32[]{:S(2)}, u32[]{:S(2)}) async-start(bf16[128,2,512]{2,1,0:T(2,128)(2,1)} %reshape.143), calls=%async_computation.3 | async-start | bytes 524288 | tf_op jit(solution)/shard_map/all_to_all | solution.py:102
  105.9 73.8 %all-to-all-start.5 = ((s32[128,1,32]{2,1,0:T(1,128)}), s32[128,1,32]{2,1,0:T(1,128)S(1)}, u32[]{:S(2)}, u32[]{:S(2)}) async-start(s32[128,1,32]{2,1,0:T(1,128)} %bitcast.26), calls=%async_computation.5 | async-start | bytes 131072 | tf_op jit(solution)/shard_map/all_to_all | solution.py:84
  116.6 58.9 %all-reduce.2.cloned.1.call-start = ((), (), s32[]{:S(2)}) async-start(), calls=%async_computation.7 | async-start | bytes 2097152 | tf_op jit(solution)/shard_map/psum | solution.py:113
  180.5 10.4 %all-to-all-start.4 = ((bf16[4,512,128]{2,1,0:T(8,128)(2,1)}), bf16[4,512,128]{2,1,0:T(8,128)(2,1)S(1)}, u32[]{:S(2)}, u32[]{:S(2)}) async-start(bf16[4,512,128]{2,1,0:T(8,128)(2,1)} %stack.2), calls=%async_computation.4 | async-start | bytes 1048576 | tf_op jit(solution)/shard_map/all_to_all | solution.py:127
  208.3 18.4 %copy-start.7 = (s32[128,16]{0,1:T(8,128)S(1)}, s32[128,16]{0,1:T(8,128)}, u32[]{:S(2)}) copy-start(s32[128,16]{0,1:T(8,128)} %param.26) | copy-start | bytes 24580
  208.3 19.5 %copy-start.4 = (bf16[512,512]{1,0:T(8,128)(2,1)S(1)}, bf16[512,512]{1,0:T(8,128)(2,1)}, u32[]{:S(2)}) copy-start(bf16[512,512]{1,0:T(8,128)(2,1)} %param.33) | copy-start | bytes 1572868
  208.3 122.1 %all-to-all-start.6 = ((bf16[128,32,512]{2,1,0:T(8,128)(2,1)}), bf16[128,32,512]{2,1,0:T(8,128)(2,1)}, u32[]{:S(2)}, u32[]{:S(2)}) async-start(bf16[128,32,512]{2,1,0:T(8,128)(2,1)} %bitcast.138), calls=%async_computation.6 | async-start | bytes 8388608 | tf_op jit(solution)/shard_map/all_to_all | solution.py:133
  340.7 3.6 copy-start.5
  351.0 13.4 %copy-start.3 = (f32[128,8,64]{2,1,0:T(8,128)S(1)}, f32[128,8,64]{2,1,0:T(8,128)}, u32[]{:S(2)}) copy-start(f32[128,8,64]{2,1,0:T(8,128)} %copy.79) | copy-start | bytes 786436
Sparse Core Ops, SparseCore 0:
  119.7 55.6 all-reduce.1
